TPU v7x, 128 devices: a whole 4x4x4 slice. The times are simulated.
128 devices in a mesh: dp: 32 (over y, z, x_hi), mp: 4 (over x_lo, core).
Axes of the slice: x: 4 (x_hi: 2, x_lo: 2; x = x_hi * 2 + x_lo), y: 4, z: 4, core: 2. Of those that a mesh axis runs over, the one named last changes fastest.
Arguments:
- tokens: bfloat16 [8192, 2048], P('dp'), may hold values from -6 to 6
- lengths: int32 [4], replicated, may hold values from 1 to 4096, 8192 in all
- w_query: float32 [2048, 2048], P('dp', 'mp')
- w_key: float32 [2048, 2048], P('dp', 'mp')
- w_value: float32 [2048, 2048], P('dp', 'mp'), may hold values from -0.125 to 0.125
- w_out: float32 [2048, 2048], P('dp', 'mp'), may hold values from -0.125 to 0.125
- w_gate: float32 [2048, 4096], P('dp', 'mp'), may hold values from -0.125 to 0.125
- w_up: float32 [2048, 4096], P('dp', 'mp'), may hold values from -0.125 to 0.125
- w_down: float32 [4096, 2048], P('dp', 'mp'), may hold values from -0.09375 to 0.09375
Outputs:
- layer_out: bfloat16 [8192, 2048], P(('dp', 'mp'))
Inputs may be any that keep to these rules, and one draw needn't show every extreme that they name: Every prompt is 1 to 4096 tokens long and one is exactly 4096; the lengths sum to 8192.
All inputs are finite; a program needn't handle non-finite values.
Results may differ from a plain program's by a relative error of at most 0.02.
The roundings to bfloat16 on the way count: a program that leaves them out, or rounds other values in their place, can miss the bound.
Values may be sent and summed in bfloat16 or wider, within the bound.
No kernel may reach another device: no remote copies, remote signals or barrier semaphores. Data moves between devices by JAX's collectives and lax.ppermute only.
A program may use at most 128 MiB of HBM per device.

v0:
```python
import jax
import jax.numpy as jnp
from jax import lax
from jax.sharding import Mesh, PartitionSpec as P

HEAD = 128
epsilon = 1e-05
theta_base = 10000.0


def shifted(value, axis, steps):
    count = lax.axis_size(axis)
    return lax.ppermute(value, axis, [(source, source + steps) for source in range(count - steps)])


def gather_by_exchange(value, axis):
    count = lax.axis_size(axis)
    copies = jnp.broadcast_to(value[None], (count,) + value.shape)
    got = lax.all_to_all(copies, axis, 0, 0, tiled=True)
    return got.reshape((count * value.shape[0],) + value.shape[1:])


def scatter_sum(value, axis):
    count = lax.axis_size(axis)
    pieces = value.reshape((count, value.shape[0] // count) + value.shape[1:])
    got = lax.all_to_all(pieces, axis, 0, 0, tiled=True)
    return jnp.sum(got.astype(jnp.float32), axis=0)


def layer_norm(rows):
    values = rows.astype(jnp.float32)
    centre = jnp.mean(values, axis=-1, keepdims=True)
    spread = jnp.mean(jnp.square(values - centre), axis=-1, keepdims=True)
    return (values - centre) * lax.rsqrt(spread + epsilon)


def prompt_coords(first, count, lengths):
    where = first + jnp.arange(count)
    ends = jnp.cumsum(lengths)
    passed = (ends[None, :] <= where[:, None]).astype(jnp.int32)
    prompt = jnp.sum(passed, axis=1)
    offset = where - jnp.sum(passed * lengths[None, :], axis=1)
    prompt = jnp.where(where < 0, -1, prompt)
    return (prompt, offset, where)


def rotate(values, offset):
    half = values.shape[-1] // 2
    freqs = jnp.power(theta_base, -jnp.arange(half, dtype=jnp.float32) * 2.0 / values.shape[-1])
    angles = offset.astype(jnp.float32)[:, None] * freqs[None, :]
    cosine = jnp.cos(angles)[:, None, :]
    sine = jnp.sin(angles)[:, None, :]
    first_half = values[..., :half]
    second_half = values[..., half:]
    return jnp.concatenate(
        [first_half * cosine - second_half * sine, second_half * cosine + first_half * sine],
        axis=-1,
    )


def on_device(tokens, lengths, w_query, w_key, w_value, w_out, w_gate, w_up, w_down):
    half_type = jnp.bfloat16
    dp = ("y", "r")
    mp = "mp"
    rows = tokens.shape[0]
    narrow = w_query.shape[1]
    shard_rows = w_query.shape[0]
    heads_dev = narrow // HEAD
    dp_index = lax.axis_index(dp)
    mp_index = lax.axis_index(mp)
    mp_size = lax.axis_size(mp)
    y_size = lax.axis_size("y")
    r_size = lax.axis_size("r")
    reach = lax.axis_size(dp) // 2
    down_rows = w_down.shape[0]
    per_mp = down_rows // mp_size
    units_shard = w_gate.shape[1]
    blocks = units_shard // down_rows

    def unit_pieces(w):
        pieces = w.astype(half_type).reshape(shard_rows, blocks, mp_size, per_mp)
        return jnp.transpose(pieces, (2, 0, 1, 3))

    outgoing = [
        unit_pieces(w_gate),
        unit_pieces(w_up),
        w_down.astype(half_type).reshape(mp_size, per_mp, narrow),
        jnp.broadcast_to(w_out.astype(half_type)[None], (mp_size,) + w_out.shape),
    ]
    flat = jnp.concatenate([p.reshape(mp_size, -1) for p in outgoing], axis=1)
    got = lax.all_to_all(flat, mp, 0, 0, tiled=True)
    kv_shard = jnp.concatenate([w.astype(half_type) for w in (w_key, w_value)], axis=1)
    got, kv_shard = lax.optimization_barrier((got, kv_shard))
    pieces = []
    at = 0
    for p in outgoing:
        size = p[0].size
        pieces.append(got[:, at : at + size].reshape(p.shape))
        at += size
    gate_got, up_got, down_got, out_got = pieces

    def unit_columns(got_w):
        return jnp.transpose(got_w, (1, 0, 2, 3)).reshape(shard_rows, mp_size * blocks * per_mp)

    gate_shard = unit_columns(gate_got)
    up_shard = unit_columns(up_got)
    down_shard = jnp.transpose(down_got, (1, 0, 2)).reshape(per_mp, mp_size * narrow)
    units = gate_shard.shape[1]
    rest_shard = jnp.concatenate(
        [w_query.astype(half_type), gate_shard, up_shard, down_shard.reshape(shard_rows, -1)],
        axis=1,
    )
    out_full_rows = jnp.transpose(out_got, (1, 0, 2)).reshape(shard_rows, mp_size * narrow)
    swap = [(a * mp_size + b, b * mp_size + a) for a in range(y_size) for b in range(mp_size)]
    out_swapped = lax.ppermute(out_full_rows, ("y", mp), swap)
    server_out = gather_by_exchange(out_swapped, "r")
    kv_full = gather_by_exchange(kv_shard, dp)
    rest_full = lax.all_gather(rest_shard, dp, axis=0, tiled=True)
    normed = layer_norm(tokens).astype(half_type)
    joined_kv = jnp.dot(normed, kv_full, preferred_element_type=jnp.float32)
    q_prompt, q_offset, q_where = prompt_coords(dp_index * rows, rows, lengths)
    shaped = joined_kv.reshape(rows, 2, heads_dev, HEAD)
    keys = rotate(shaped[:, 0], q_offset).astype(half_type)
    values = shaped[:, 1].astype(half_type)
    own_pair = jnp.transpose(jnp.stack((keys, values)), (0, 2, 1, 3))
    plane = r_size
    back_one = shifted(own_pair, dp, plane)
    back_two = shifted(own_pair, dp, 2 * plane)
    own_first = dp_index * rows
    scale = 1.0 / HEAD**0.5

    def online_step(state, pair, first):
        accum, total, top = state
        k_prompt, k_offset, k_where = prompt_coords(first, rows, lengths)
        scores = (
            jnp.einsum("hqd,hkd->hqk", query, pair[0], preferred_element_type=jnp.float32) * scale
        )
        allowed = (q_prompt[:, None] == k_prompt[None, :]) & (k_where[None, :] <= q_where[:, None])
        scores = jnp.where(allowed[None], scores, -jnp.inf)
        new_top = jnp.maximum(top, jnp.max(scores, axis=-1, keepdims=True))
        fade = jnp.exp(top - new_top)
        weights = jnp.exp(scores - new_top)
        probs = weights.astype(half_type)
        product = jnp.einsum("hqk,hkd->hqd", probs, pair[1], preferred_element_type=jnp.float32)
        accum = accum * fade + product
        total = total * fade + jnp.sum(weights, axis=-1, keepdims=True)
        return (accum, total, new_top)

    state = (
        jnp.zeros((heads_dev, rows, HEAD), jnp.float32),
        jnp.zeros((heads_dev, rows, 1), jnp.float32),
        jnp.full((heads_dev, rows, 1), -jnp.inf, jnp.float32),
    )
    r_index = lax.axis_index("r")
    later = r_index < jnp.arange(plane)
    nearer = jnp.where(later[:, None, None, None, None], own_pair[None], back_two[None])
    payload = jnp.stack(
        (nearer, jnp.broadcast_to(back_one[None], (plane,) + back_one.shape)), axis=1
    )
    received = lax.all_to_all(payload, "r", 0, 0, tiled=True)
    q_full = rest_full[:, :narrow]
    server_gate = rest_full[:, narrow : narrow + units]
    server_up = rest_full[:, narrow + units : narrow + 2 * units]
    server_down = rest_full[:, narrow + 2 * units :].reshape(units, -1)
    received, q_full, server_gate, server_up, server_down = lax.optimization_barrier(
        (received, q_full, server_gate, server_up, server_down)
    )
    joined_q = jnp.dot(normed, q_full, preferred_element_type=jnp.float32)
    query = rotate(joined_q.reshape(rows, heads_dev, HEAD), q_offset).astype(half_type)
    query = jnp.transpose(query, (1, 0, 2))
    state = online_step(state, own_pair, own_first)

    def slot_step(back, state):
        source = lax.rem(r_index - back + 2 * plane, plane)
        middle = jnp.logical_and(back > r_index, back <= r_index + plane).astype(jnp.int32)
        pair = received[source, middle]
        return online_step(state, pair, own_first - back * rows)

    state = lax.fori_loop(1, reach + 1, slot_step, state)
    accum, total, top = state
    context = jnp.transpose((accum / total).astype(half_type), (1, 0, 2)).reshape(rows, narrow)
    partial_out = jnp.dot(context, server_out, preferred_element_type=jnp.float32)
    attended = scatter_sum(partial_out.astype(half_type), mp)
    slab = rows // mp_size
    own_tokens = lax.dynamic_slice_in_dim(tokens, mp_index * slab, slab, 0)
    mixed = (own_tokens.astype(jnp.float32) + attended).astype(half_type)
    normed_own = layer_norm(mixed).astype(half_type)
    normed_two = gather_by_exchange(normed_own, mp)
    gate = jnp.dot(normed_two, server_gate, preferred_element_type=jnp.float32)
    upper = jnp.dot(normed_two, server_up, preferred_element_type=jnp.float32)
    hidden = (jax.nn.silu(gate) * upper).astype(half_type)
    partial_down = jnp.dot(hidden, server_down, preferred_element_type=jnp.float32)
    share = scatter_sum(partial_down.astype(half_type), mp)
    return (mixed.astype(jnp.float32) + share).astype(half_type)


def solution(mesh):
    dp_size, mp_size = mesh.devices.shape
    y_size = mesh.devices.shape[0] // 8 if dp_size % 8 == 0 else 1
    fine = Mesh(mesh.devices.reshape(y_size, dp_size // y_size, mp_size), ("y", "r", "mp"))
    dp = ("y", "r")
    in_specs = (
        P(dp, None),
        P(),
        P(dp, "mp"),
        P(dp, "mp"),
        P(dp, "mp"),
        P(dp, "mp"),
        P(dp, "mp"),
        P(dp, "mp"),
        P(dp, "mp"),
    )
    out_specs = P(("y", "r", "mp"), None)
    return jax.shard_map(
        on_device, mesh=fine, in_specs=in_specs, out_specs=out_specs, check_vma=False
    )
```

profile of v0, /device:TPU:1, one launch (start us, length us, event | category | flops | bytes accessed | tf_op | source)
XLA Modules:
  0.0 446.5 jit_solution(5128202686256242654)
XLA Ops:
  12.6 1.5 reduce
  14.1 1.5 reshape.429
  15.6 4.9 %all-to-all-start = ((bf16[4,2,40960]{2,1,0:T(2,128)(2,1)}), bf16[4,2,40960]{2,1,0:T(2,128)(2,1)S(1)}, u32[]{:S(2)}, u32[]{:S(2)}) async-start(bf16[4,2,40960]{2,1,0:T(2,128)(2,1)} %reshape.429), calls=%async_computation | async-start | bytes 1310720 | tf_op jit(solution)/shard_map/all_to_all | solution.py:91
  20.7 9.2 %all-to-all-done = bf16[4,2,40960]{2,1,0:T(2,128)(2,1)S(1)} async-done(((bf16[4,2,40960]{2,1,0:T(2,128)(2,1)}), bf16[4,2,40960]{2,1,0:T(2,128)(2,1)S(1)}, u32[]{:S(2)}, u32[]{:S(2)}) %all-to-all-start) | async-done | bytes 655392 | tf_op jit(solution)/shard_map/all_to_all | solution.py:91
  34.4 2.6 broadcast_in_dim.188
  36.9 10.9 %all-to-all-start.1 = ((bf16[32,64,1024]{2,1,0:T(8,128)(2,1)}), bf16[32,64,1024]{2,1,0:T(8,128)(2,1)}, u32[]{:S(2)}, u32[]{:S(2)}) async-start(bf16[32,64,1024]{2,1,0:T(8,128)(2,1)} %broadcast_in_dim.188), calls=%async_computation.1 | async-start | bytes 8388608 | tf_op jit(solution)/shard_map/all_to_all | solution.py:19
  49.1 64.7 %all-to-all-done.1 = bf16[32,64,1024]{2,1,0:T(8,128)(2,1)} async-done(((bf16[32,64,1024]{2,1,0:T(8,128)(2,1)}), bf16[32,64,1024]{2,1,0:T(8,128)(2,1)}, u32[]{:S(2)}, u32[]{:S(2)}) %all-to-all-start.1) | async-done | bytes 4194336 | tf_op jit(solution)/shard_map/all_to_all | solution.py:19
  113.8 6.5 %copy.139 = bf16[1024,2048]{1,0:T(8,128)(2,1)} copy(bf16[1024,2048]{0,1:T(8,128)(2,1)} %bitcast.10) | data formatting | bytes 8388608 | tf_op jit(solution)/shard_map/dot_general | solution.py:120
  120.3 3.6 fusion.17
  124.1 3.0 collective-permute-start.1
  127.1 1.5 collective-permute-start
  129.6 11.8 %collective-permute-done.1 = bf16[2,4,256,128]{2,3,1,0:T(8,128)(2,1)} collective-permute-done((bf16[2,4,256,128]{2,3,1,0:T(8,128)(2,1)S(1)}, bf16[2,4,256,128]{2,3,1,0:T(8,128)(2,1)}, u32[]{:S(2)}, u32[]{:S(2)}) %collective-permute-start.1) | collective-permute-done | bytes 524320 | tf_op jit(solution)/shard_map/ppermute | solution.py:13
  141.5 2.1 copy.142
  143.5 9.2 %collective-permute-done = bf16[2,4,256,128]{2,3,1,0:T(8,128)(2,1)S(1)} collective-permute-done((bf16[2,4,256,128]{2,3,1,0:T(8,128)(2,1)S(1)}, bf16[2,4,256,128]{2,3,1,0:T(8,128)(2,1)S(1)}, u32[]{:S(2)}, u32[]{:S(2)}) %collective-permute-start) | collective-permute-done | bytes 524320 | tf_op jit(solution)/shard_map/ppermute | solution.py:13
  153.7 1.8 broadcast_select_fusion
  155.5 3.0 stack_broadcast_in_dim.2
  158.5 6.8 %pad_maximum_fusion = bf16[8,2,2,4,256,128]{5,4,3,2,1,0:T(8,128)(2,1)} fusion(bf16[8,1,2,4,256,128]{5,4,3,2,1,0:T(8,128)(2,1)} %stack_broadcast_in_dim.2, bf16[8,1,2,4,256,128]{5,4,3,2,1,0:T(8,128)(2,1)S(1)} %broadcast_select_fusion), kind=kLoop, calls=%fused_computation.22 | loop fusion | flops 4194304 | bytes 16777216 | tf_op jit(solution)/shard_map/stack | solution.py:157
  165.3 5.0 %all-to-all-start.2 = ((bf16[8,2,2,4,256,128]{5,4,3,2,1,0:T(8,128)(2,1)}), bf16[8,2,2,4,256,128]{5,4,3,2,1,0:T(8,128)(2,1)}, u32[]{:S(2)}, u32[]{:S(2)}) async-start(bf16[8,2,2,4,256,128]{5,4,3,2,1,0:T(8,128)(2,1)} %pad_maximum_fusion), calls=%async_computation.2 | async-start | bytes 16777216 | tf_op jit(solution)/shard_map/all_to_all | solution.py:160
  170.6 4.8 %collective-permute-start.2 = (bf16[64,2048]{1,0:T(8,128)(2,1)S(1)}, bf16[64,2048]{1,0:T(8,128)(2,1)S(1)}, u32[]{:S(2)}, u32[]{:S(2)}) collective-permute-start(bf16[64,2048]{1,0:T(8,128)(2,1)S(1)} %bitcast.142), channel_id=1, source_target_pairs={{0,0},{1,32},{2,64},{3,96},{32,1},{33,33},{34,65},{35,97},{64,2},{... | collective-permute-start | bytes 786440 | tf_op jit(solution)/shard_map/ppermute | solution.py:115
  175.4 122.5 %all-gather.2.cloned.1.call-done = bf16[2048,3584]{1,0:T(8,128)(2,1)} async-done(((bf16[64,3584]{1,0:T(8,128)(2,1)}), bf16[2048,3584]{1,0:T(8,128)(2,1)}) %all-gather.2.cloned.1.call-update) | async-done | bytes 14680080 | tf_op jit(solution)/shard_map/all_gather | solution.py:118
  297.9 9.1 %fusion.39 = (bf16[2048,1024]{1,0:T(8,128)(2,1)}, bf16[2048,1024]{1,0:T(8,128)(2,1)}, bf16[2048,1024]{1,0:T(8,128)(2,1)}) fusion(bf16[2048,3584]{1,0:T(8,128)(2,1)} %all-gather.2.cloned.1.call-done), kind=kLoop, calls=%fused_computation.95 | loop fusion | bytes 25165824 | tf_op jit(solution)/shard_map/slice | solution.py:164
  307.0 7.1 %reshape.418 = bf16[1024,2048]{1,0:T(8,128)(2,1)} reshape(bf16[2048,1024]{1,0:T(8,128)(2,1)} %get-tuple-element.444) | data formatting | bytes 8388608 | tf_op jit(solution)/shard_map/reshape | solution.py:164
  314.1 1.7 broadcast_in_dim.195
  315.7 4.5 %all-to-all-start.3 = ((bf16[8,64,2048]{2,1,0:T(8,128)(2,1)}), bf16[8,64,2048]{2,1,0:T(8,128)(2,1)}, u32[]{:S(2)}, u32[]{:S(2)}) async-start(bf16[8,64,2048]{2,1,0:T(8,128)(2,1)} %broadcast_in_dim.195), calls=%async_computation.3 | async-start | bytes 4194304 | tf_op jit(solution)/shard_map/all_to_all | solution.py:19
  324.4 51.2 %while.21 = (s32[]{:T(128)}, f32[4,256,128]{2,1,0:T(8,128)S(1)}, f32[4,256,1]{1,0,2:T(4,128)S(1)}, f32[4,256,1]{1,0,2:T(4,128)S(1)}, s32[256]{0:T(256)S(1)}, /*i...) while((s32[]{:T(128)}, f32[4,256,128]{2,1,0:T(8,128)S(1)}, ...), condition=%wide.region_11.12_spmd.clone.clone, body=%wide.region_7.11_spmd.clone.clone.sunk | while | flops 136518688 | bytes 5188022 | solution.py:179
  329.4 1.4 convolution_add_fusion.3
  376.0 3.4 convolution_convert_fusion
  379.4 3.9 all-to-all-start.4
  383.3 13.6 %all-to-all-done.4 = bf16[4,64,2048]{2,1,0:T(8,128)(2,1)S(1)} async-done(((bf16[4,64,2048]{2,1,0:T(8,128)(2,1)}), bf16[4,64,2048]{2,1,0:T(8,128)(2,1)S(1)}, u32[]{:S(2)}, u32[]{:S(2)}) %all-to-all-start.4) | async-done | bytes 1048608 | tf_op jit(solution)/shard_map/all_to_all | solution.py:26
  397.8 16.8 %all_to_all.42 = bf16[4,64,2048]{2,1,0:T(8,128)(2,1)S(1)} all-to-all(bf16[4,64,2048]{2,1,0:T(8,128)(2,1)S(1)} %broadcast_in_dim.196), channel_id=1, replica_groups=mesh['y'=4,'r'=8,'mp'=4] {'mp'}, dimensions={0} | all-to-all | bytes 2097152 | tf_op jit(solution)/shard_map/all_to_all | solution.py:19
  415.9 5.9 %convolution_convert_fusion.1 = bf16[256,2048]{1,0:T(8,128)(2,1)S(1)} fusion(bf16[1024,2048]{1,0:T(8,128)(2,1)} %reshape.418, bf16[256,2048]{1,0:T(8,128)(2,1)S(1)} %bitcast.134, bf16[2048,1024]{1,0:T(8,128)(2,1)} %get-tuple-element.280, f32[256,1024]{1,0:T(8,128)S(1)} %fusion.42), kind=kOutput, calls=%fused_computation.27 | convolution fusion | flops 2149580800 | bytes 11534336 | tf_op jit(solution)/shard_map/dot_general | solution.py:192
  421.8 16.9 %all_to_all.43 = bf16[4,64,2048]{2,1,0:T(8,128)(2,1)S(1)} all-to-all(bf16[4,64,2048]{2,1,0:T(8,128)(2,1)S(1)} %bitcast.135), channel_id=1, replica_groups=mesh['y'=4,'r'=8,'mp'=4] {'mp'}, dimensions={0} | all-to-all | bytes 2097152 | tf_op jit(solution)/shard_map/all_to_all | solution.py:26
  (254 shorter events, 70.1 us)
Async XLA Ops:
  6.5 4.1 copy-start.4
  12.1 8.4 %copy-start.5 = (f32[64,512]{1,0:T(8,128)S(1)}, f32[64,512]{1,0:T(8,128)}, u32[]{:S(2)}) copy-start(f32[64,512]{1,0:T(8,128)} %param.13) | copy-start | bytes 393220
  12.6 8.1 %copy-start.6 = (f32[64,512]{1,0:T(8,128)S(1)}, f32[64,512]{1,0:T(8,128)}, u32[]{:S(2)}) copy-start(f32[64,512]{1,0:T(8,128)} %param.14) | copy-start | bytes 393220
  12.6 8.1 %copy-start.7 = (f32[64,512]{1,0:T(8,128)S(1)}, f32[64,512]{1,0:T(8,128)}, u32[]{:S(2)}) copy-start(f32[64,512]{1,0:T(8,128)} %param.15) | copy-start | bytes 393220
  15.6 14.3 %all-to-all-start = ((bf16[4,2,40960]{2,1,0:T(2,128)(2,1)}), bf16[4,2,40960]{2,1,0:T(2,128)(2,1)S(1)}, u32[]{:S(2)}, u32[]{:S(2)}) async-start(bf16[4,2,40960]{2,1,0:T(2,128)(2,1)} %reshape.429), calls=%async_computation | async-start | bytes 1310720 | tf_op jit(solution)/shard_map/all_to_all | solution.py:91
  20.5 277.4 %all-gather.2.cloned.1.call-start = ((), (), s32[]{:S(2)}) async-start(), calls=%async_computation.7 | async-start | bytes 15138816 | tf_op jit(solution)/shard_map/all_gather | solution.py:118
  36.9 10.9 %copy-start.8 = (s32[4]{0:T(128)S(1)}, s32[4]{0:T(128)}, u32[]{:S(2)}) copy-start(s32[4]{0:T(128)} %param.12) | copy-start | bytes 52
  36.9 11.2 %copy-start = (bf16[256,2048]{1,0:T(8,128)(2,1)S(1)}, bf16[256,2048]{1,0:T(8,128)(2,1)}, u32[]{:S(2)}) copy-start(bf16[256,2048]{1,0:T(8,128)(2,1)} %param.11) | copy-start | bytes 3145732
  36.9 76.8 %all-to-all-start.1 = ((bf16[32,64,1024]{2,1,0:T(8,128)(2,1)}), bf16[32,64,1024]{2,1,0:T(8,128)(2,1)}, u32[]{:S(2)}, u32[]{:S(2)}) async-start(bf16[32,64,1024]{2,1,0:T(8,128)(2,1)} %broadcast_in_dim.188), calls=%async_computation.1 | async-start | bytes 8388608 | tf_op jit(solution)/shard_map/all_to_all | solution.py:19
  124.1 28.6 %copy-start.2 = (bf16[2,4,256,128]{2,3,1,0:T(8,128)(2,1)}, bf16[2,4,256,128]{2,3,1,0:T(8,128)(2,1)S(1)}, u32[]{:S(2)}) copy-start(bf16[2,4,256,128]{2,3,1,0:T(8,128)(2,1)S(1)} %maximum_bitcast_fusion.1) | copy-start | bytes 1572868
  124.1 17.4 %collective-permute-start.1 = (bf16[2,4,256,128]{2,3,1,0:T(8,128)(2,1)S(1)}, bf16[2,4,256,128]{2,3,1,0:T(8,128)(2,1)}, u32[]{:S(2)}, u32[]{:S(2)}) collective-permute-start(bf16[2,4,256,128]{2,3,1,0:T(8,128)(2,1)S(1)} %maximum_bitcast_fusion.1), channel_id=1, source_target_pairs={{0,32},{4,36},{8,40},{12,44},{16,48},{20,52},{24,56},{28,60},{32,6... | collective-permute-start | bytes 1572872 | tf_op jit(solution)/shard_map/ppermute | solution.py:13
  127.1 25.6 %collective-permute-start = (bf16[2,4,256,128]{2,3,1,0:T(8,128)(2,1)S(1)}, bf16[2,4,256,128]{2,3,1,0:T(8,128)(2,1)S(1)}, u32[]{:S(2)}, u32[]{:S(2)}) collective-permute-start(bf16[2,4,256,128]{2,3,1,0:T(8,128)(2,1)S(1)} %maximum_bitcast_fusion.1), channel_id=1, source_target_pairs={{0,64},{4,68},{8,72},{12,76},{16,80},{20,84},{24,88},{28,92},{32,9... | collective-permute-start | bytes 1572872 | tf_op jit(solution)/shard_map/ppermute | solution.py:13
  153.7 1.8 copy-start.3
  165.3 148.8 %all-to-all-start.2 = ((bf16[8,2,2,4,256,128]{5,4,3,2,1,0:T(8,128)(2,1)}), bf16[8,2,2,4,256,128]{5,4,3,2,1,0:T(8,128)(2,1)}, u32[]{:S(2)}, u32[]{:S(2)}) async-start(bf16[8,2,2,4,256,128]{5,4,3,2,1,0:T(8,128)(2,1)} %pad_maximum_fusion), calls=%async_computation.2 | async-start | bytes 16777216 | tf_op jit(solution)/shard_map/all_to_all | solution.py:160
  170.6 143.5 %collective-permute-start.2 = (bf16[64,2048]{1,0:T(8,128)(2,1)S(1)}, bf16[64,2048]{1,0:T(8,128)(2,1)S(1)}, u32[]{:S(2)}, u32[]{:S(2)}) collective-permute-start(bf16[64,2048]{1,0:T(8,128)(2,1)S(1)} %bitcast.142), channel_id=1, source_target_pairs={{0,0},{1,32},{2,64},{3,96},{32,1},{33,33},{34,65},{35,97},{64,2},{... | collective-permute-start | bytes 786440 | tf_op jit(solution)/shard_map/ppermute | solution.py:115
  315.7 4.5 %slice-start = ((bf16[2048,3584]{1,0:T(8,128)(2,1)}), bf16[2048,512]{1,0:T(8,128)(2,1)S(1)}, s32[]{:S(2)}) async-start(bf16[2048,3584]{1,0:T(8,128)(2,1)} %all-gather.2.cloned.1.call-done), calls=%async_computation.8 | async-start | bytes 4194304 | tf_op jit(solution)/shard_map/slice | solution.py:161
  315.7 60.2 %all-to-all-start.3 = ((bf16[8,64,2048]{2,1,0:T(8,128)(2,1)}), bf16[8,64,2048]{2,1,0:T(8,128)(2,1)}, u32[]{:S(2)}, u32[]{:S(2)}) async-start(bf16[8,64,2048]{2,1,0:T(8,128)(2,1)} %broadcast_in_dim.195), calls=%async_computation.3 | async-start | bytes 4194304 | tf_op jit(solution)/shard_map/all_to_all | solution.py:19
  379.4 17.5 %all-to-all-start.4 = ((bf16[4,64,2048]{2,1,0:T(8,128)(2,1)}), bf16[4,64,2048]{2,1,0:T(8,128)(2,1)S(1)}, u32[]{:S(2)}, u32[]{:S(2)}) async-start(bf16[4,64,2048]{2,1,0:T(8,128)(2,1)} %bitcast.35), calls=%async_computation.4 | async-start | bytes 2097152 | tf_op jit(solution)/shard_map/all_to_all | solution.py:26
  397.2 17.4 %copy-start.1 = (bf16[2048,1024]{1,0:T(8,128)(2,1)S(1)}, bf16[2048,1024]{1,0:T(8,128)(2,1)}, u32[]{:S(2)}) copy-start(bf16[2048,1024]{1,0:T(8,128)(2,1)} %get-tuple-element.279) | copy-start | bytes 12582916
Sparse Core Ops, SparseCore 0:
  34.5 263.3 all-gather.1
where the time goes:
time: 449 us; the launch traced here: 446 us
  waiting for transfers between devices  231 us (51%)
  matrix products  60.9 us (14%)
  local copies, waits for them, and re-layouts  44.3 us (10%)
  starting transfers between devices  38.4 us (9%)
  blocking collectives  33.7 us (8%)
  other arithmetic  22.8 us (5%)
  between operations  13.9 us (3%)
    all_gather x1, waiting for transfers between devices, on_device(): rest_full = lax.all_gather(rest_shard, dp, axis=0, tiled=True)  123 us
    all_to_all x2, waiting for transfers between devices, gather_by_exchange(): got = lax.all_to_all(copies, axis, 0, 0, tiled=True)  64.7 us
    dot_general x17, matrix products, online_step(): jnp.einsum('hqk,hkd->hqd', probs, pair[1], preferred_element_type=jnp.flo...  24 us
    dot_general x17, matrix products, online_step(): jnp.einsum('hqd,hkd->hqk', query, pair[0], preferred_element_type=jnp.flo...  21.7 us
    ppermute x2, waiting for transfers between devices, shifted(): lax.ppermute(value, axis, [(source, source + steps) for source in range(c...  21 us
    all_to_all x1, blocking collectives, scatter_sum(): got = lax.all_to_all(pieces, axis, 0, 0, tiled=True)  16.9 us
    all_to_all x1, blocking collectives, gather_by_exchange(): got = lax.all_to_all(copies, axis, 0, 0, tiled=True)  16.8 us
    all_to_all x2, starting transfers between devices, gather_by_exchange(): got = lax.all_to_all(copies, axis, 0, 0, tiled=True)  15.3 us
  transfers between devices with their start and end apart: 9, of which 6 were waited for; matrix products, arithmetic and copies ran while one was open for 23% of the time, Pallas kernels for 0%

commit v1 on v0

--- a/solution.py
+++ b/solution.py
@@ -115,7 +115,8 @@
     out_swapped = lax.ppermute(out_full_rows, ("y", mp), swap)
     server_out = gather_by_exchange(out_swapped, "r")
     kv_full = gather_by_exchange(kv_shard, dp)
-    rest_full = lax.all_gather(rest_shard, dp, axis=0, tiled=True)
+    sent = jnp.stack([rest_shard] * lax.axis_size(dp))
+    rest_full = jnp.concatenate(lax.all_to_all(sent, dp, 0, 0), axis=0)
     normed = layer_norm(tokens).astype(half_type)
     joined_kv = jnp.dot(normed, kv_full, preferred_element_type=jnp.float32)
     q_prompt, q_offset, q_where = prompt_coords(dp_index * rows, rows, lengths)

time: 449 us -> 607 us (1.35)
  waiting for transfers between devices: 231 us -> 368 us
  starting transfers between devices: 38.4 us -> 60.5 us
  between operations: 13.9 us -> 0.54 us
  local copies, waits for them, and re-layouts: 44.3 us -> 54.4 us
    ppermute x2, waiting for transfers between devices: 21 us -> 219 us  [shifted(): lax.ppermute(value, axis, [(source, source + steps) for source in range(c...]
    all_gather x1 -> x0, waiting for transfers between devices: 123 us -> none  [on_device(): rest_full = lax.all_gather(rest_shard, dp, axis=0, tiled=True)]
    all_to_all x1, waiting for transfers between devices: 0.01 us -> 71 us  [on_device(): received = lax.all_to_all(payload, 'r', 0, 0, tiled=True)]
    all_to_all x1, starting transfers between devices: 3.94 us -> 19.4 us  [scatter_sum(): got = lax.all_to_all(pieces, axis, 0, 0, tiled=True)]
    all_to_all x2, waiting for transfers between devices: 64.7 us -> 55.4 us  [gather_by_exchange(): got = lax.all_to_all(copies, axis, 0, 0, tiled=True)]
    another operation x0 -> x1, local copies, waits for them, and re-layouts: none -> 6.85 us  [on_device(): sent = jnp.stack([rest_shard] * lax.axis_size(dp))]
  transfers between devices with their start and end apart: 9 -> 9, of which waited for: 6 -> 6; matrix products, arithmetic and copies ran while one was open for 23% -> 17% of each run, Pallas kernels for 0% -> 0%
where the time goes in v1:
time: 607 us; the launch traced here: 602 us
  waiting for transfers between devices  368 us (61%)
  starting transfers between devices  60.5 us (10%)
  matrix products  60.4 us (10%)
  local copies, waits for them, and re-layouts  54.4 us (9%)
  blocking collectives  34 us (6%)
  other arithmetic  22 us (4%)
    ppermute x2, waiting for transfers between devices, shifted(): lax.ppermute(value, axis, [(source, source + steps) for source in range(c...  219 us
    all_to_all x1, waiting for transfers between devices, on_device(): received = lax.all_to_all(payload, 'r', 0, 0, tiled=True)  71 us
    all_to_all x2, waiting for transfers between devices, gather_by_exchange(): got = lax.all_to_all(copies, axis, 0, 0, tiled=True)  55.4 us
    dot_general x17, matrix products, online_step(): jnp.einsum('hqk,hkd->hqd', probs, pair[1], preferred_element_type=jnp.flo...  23 us
    dot_general x17, matrix products, online_step(): jnp.einsum('hqd,hkd->hqk', query, pair[0], preferred_element_type=jnp.flo...  20.7 us
    all_to_all x1, starting transfers between devices, scatter_sum(): got = lax.all_to_all(pieces, axis, 0, 0, tiled=True)  19.4 us
    all_to_all x1, blocking collectives, gather_by_exchange(): got = lax.all_to_all(copies, axis, 0, 0, tiled=True)  17.1 us
    all_to_all x1, blocking collectives, scatter_sum(): got = lax.all_to_all(pieces, axis, 0, 0, tiled=True)  16.9 us
  transfers between devices with their start and end apart: 9, of which 6 were waited for; matrix products, arithmetic and copies ran while one was open for 17% of the time, Pallas kernels for 0%

profile of v1, /device:TPU:1, one launch (start us, length us, event | category | flops | bytes accessed | tf_op | source)
XLA Modules:
  0.0 601.6 jit_solution(16259104194180619939)
XLA Ops:
  8.2 4.9 all-to-all-start
  13.3 9.2 %all-to-all-done = bf16[4,2,40960]{2,1,0:T(2,128)(2,1)S(1)} async-done(((bf16[4,2,40960]{2,1,0:T(2,128)(2,1)}), bf16[4,2,40960]{2,1,0:T(2,128)(2,1)S(1)}, u32[]{:S(2)}, u32[]{:S(2)}) %all-to-all-start) | async-done | bytes 655392 | tf_op jit(solution)/shard_map/all_to_all | solution.py:91
  24.0 2.5 broadcast_in_dim.188
  26.4 10.7 %all-to-all-start.1 = ((bf16[32,64,1024]{2,1,0:T(8,128)(2,1)}), bf16[32,64,1024]{2,1,0:T(8,128)(2,1)}, u32[]{:S(2)}, u32[]{:S(2)}) async-start(bf16[32,64,1024]{2,1,0:T(8,128)(2,1)} %broadcast_in_dim.188), calls=%async_computation.1 | async-start | bytes 8388608 | tf_op jit(solution)/shard_map/all_to_all | solution.py:19
  39.4 55.4 %all-to-all-done.1 = bf16[32,64,1024]{2,1,0:T(8,128)(2,1)} async-done(((bf16[32,64,1024]{2,1,0:T(8,128)(2,1)}), bf16[32,64,1024]{2,1,0:T(8,128)(2,1)}, u32[]{:S(2)}, u32[]{:S(2)}) %all-to-all-start.1) | async-done | bytes 4194336 | tf_op jit(solution)/shard_map/all_to_all | solution.py:19
  94.7 6.8 %stack.8 = bf16[32,64,3584]{2,1,0:T(8,128)(2,1)} broadcast(bf16[64,3584]{1,0:T(8,128)(2,1)S(1)} %copy.128), dimensions={1,2} | broadcast | bytes 15138816 | tf_op jit(solution)/shard_map/stack | solution.py:118
  101.6 6.0 all-to-all-start.3
  108.8 6.5 %copy.119 = bf16[1024,2048]{1,0:T(8,128)(2,1)} copy(bf16[1024,2048]{0,1:T(8,128)(2,1)} %bitcast.10) | data formatting | bytes 8388608 | tf_op jit(solution)/shard_map/dot_general | solution.py:121
  115.4 3.6 fusion.17
  119.1 3.8 collective-permute-start.1
  122.9 3.5 collective-permute-start
  127.5 209.5 %collective-permute-done.1 = bf16[2,4,256,128]{2,3,1,0:T(8,128)(2,1)} collective-permute-done((bf16[2,4,256,128]{2,3,1,0:T(8,128)(2,1)S(1)}, bf16[2,4,256,128]{2,3,1,0:T(8,128)(2,1)}, u32[]{:S(2)}, u32[]{:S(2)}) %collective-permute-start.1) | collective-permute-done | bytes 524320 | tf_op jit(solution)/shard_map/ppermute | solution.py:13
  338.2 9.9 %collective-permute-done = bf16[2,4,256,128]{2,3,1,0:T(8,128)(2,1)S(1)} collective-permute-done((bf16[2,4,256,128]{2,3,1,0:T(8,128)(2,1)S(1)}, bf16[2,4,256,128]{2,3,1,0:T(8,128)(2,1)S(1)}, u32[]{:S(2)}, u32[]{:S(2)}) %collective-permute-start) | collective-permute-done | bytes 524320 | tf_op jit(solution)/shard_map/ppermute | solution.py:13
  349.2 1.7 broadcast_select_fusion
  350.9 3.0 stack_broadcast_in_dim.2
  353.9 6.3 %pad_maximum_fusion = bf16[8,2,2,4,256,128]{5,4,3,2,1,0:T(8,128)(2,1)} fusion(bf16[8,1,2,4,256,128]{5,4,3,2,1,0:T(8,128)(2,1)} %stack_broadcast_in_dim.2, bf16[8,1,2,4,256,128]{5,4,3,2,1,0:T(8,128)(2,1)S(1)} %broadcast_select_fusion), kind=kLoop, calls=%fused_computation.22 | loop fusion | flops 4194304 | bytes 16777216 | tf_op jit(solution)/shard_map/stack | solution.py:158
  360.2 5.0 all-to-all-start.2
  366.4 1.9 collective-permute-start.2
  368.3 9.1 %fusion.39 = (bf16[2048,1024]{1,0:T(8,128)(2,1)}, bf16[2048,1024]{1,0:T(8,128)(2,1)}, bf16[2048,1024]{1,0:T(8,128)(2,1)}) fusion(bf16[2048,3584]{1,0:T(8,128)(2,1)} %bitcast.23), kind=kLoop, calls=%fused_computation.95 | loop fusion | bytes 25165824 | tf_op jit(solution)/shard_map/slice | solution.py:165
  377.4 3.0 slice.93
  380.4 7.1 %reshape.424 = bf16[1024,2048]{1,0:T(8,128)(2,1)} reshape(bf16[2048,1024]{1,0:T(8,128)(2,1)} %get-tuple-element.433) | data formatting | bytes 8388608 | tf_op jit(solution)/shard_map/reshape | solution.py:165
  387.6 71.0 %all-to-all-done.2 = bf16[8,2,2,4,256,128]{5,4,3,2,1,0:T(8,128)(2,1)} async-done(((bf16[8,2,2,4,256,128]{5,4,3,2,1,0:T(8,128)(2,1)}), bf16[8,2,2,4,256,128]{5,4,3,2,1,0:T(8,128)(2,1)}, u32[]{:S(2)}, u32[]{:S(2)}) %all-to-all-start.2) | async-done | bytes 8388640 | tf_op jit(solution)/shard_map/all_to_all | solution.py:161
  458.5 1.6 broadcast_in_dim.195
  460.1 5.4 all-to-all-start.4
  465.5 2.6 fusion.35
  471.0 51.2 %while.21 = (s32[]{:T(128)}, f32[4,256,128]{2,1,0:T(8,128)S(1)}, f32[4,256,1]{1,0,2:T(4,128)S(1)}, f32[4,256,1]{1,0,2:T(4,128)S(1)}, s32[256]{0:T(256)S(1)}, /*i...) while((s32[]{:T(128)}, f32[4,256,128]{2,1,0:T(8,128)S(1)}, ...), condition=%wide.region_11.12_spmd.clone.clone, body=%wide.region_7.11_spmd.clone.clone.sunk | while | flops 136518688 | bytes 5188022 | solution.py:180
  522.6 3.3 convolution_convert_fusion
  525.9 19.4 %all-to-all-start.5 = ((bf16[4,64,2048]{2,1,0:T(8,128)(2,1)}), bf16[4,64,2048]{2,1,0:T(8,128)(2,1)S(1)}, u32[]{:S(2)}, u32[]{:S(2)}) async-start(bf16[4,64,2048]{2,1,0:T(8,128)(2,1)} %bitcast.124), calls=%async_computation.5 | async-start | bytes 2097152 | tf_op jit(solution)/shard_map/all_to_all | solution.py:26
  545.2 13.4 %all-to-all-done.5 = bf16[4,64,2048]{2,1,0:T(8,128)(2,1)S(1)} async-done(((bf16[4,64,2048]{2,1,0:T(8,128)(2,1)}), bf16[4,64,2048]{2,1,0:T(8,128)(2,1)S(1)}, u32[]{:S(2)}, u32[]{:S(2)}) %all-to-all-start.5) | async-done | bytes 1048608 | tf_op jit(solution)/shard_map/all_to_all | solution.py:26
  559.5 17.1 %all_to_all.47 = bf16[4,64,2048]{2,1,0:T(8,128)(2,1)S(1)} all-to-all(bf16[4,64,2048]{2,1,0:T(8,128)(2,1)S(1)} %broadcast_in_dim.196), channel_id=1, replica_groups=mesh['y'=4,'r'=8,'mp'=4] {'mp'}, dimensions={0} | all-to-all | bytes 2097152 | tf_op jit(solution)/shard_map/all_to_all | solution.py:19
  577.8 5.9 convolution_convert_fusion.1
  583.8 16.9 %all_to_all.48 = bf16[4,64,2048]{2,1,0:T(8,128)(2,1)S(1)} all-to-all(bf16[4,64,2048]{2,1,0:T(8,128)(2,1)S(1)} %bitcast.137), channel_id=1, replica_groups=mesh['y'=4,'r'=8,'mp'=4] {'mp'}, dimensions={0} | all-to-all | bytes 2097152 | tf_op jit(solution)/shard_map/all_to_all | solution.py:26
  (253 shorter events, 73.9 us)
Async XLA Ops:
  0.0 3.1 copy-start.3
  1.0 3.2 copy-start.4
  4.6 8.4 %copy-start.5 = (f32[64,512]{1,0:T(8,128)S(1)}, f32[64,512]{1,0:T(8,128)}, u32[]{:S(2)}) copy-start(f32[64,512]{1,0:T(8,128)} %param.15) | copy-start | bytes 393220
  4.7 8.5 %copy-start.6 = (f32[64,512]{1,0:T(8,128)S(1)}, f32[64,512]{1,0:T(8,128)}, u32[]{:S(2)}) copy-start(f32[64,512]{1,0:T(8,128)} %param.14) | copy-start | bytes 393220
  5.2 8.0 %copy-start.7 = (f32[64,512]{1,0:T(8,128)S(1)}, f32[64,512]{1,0:T(8,128)}, u32[]{:S(2)}) copy-start(f32[64,512]{1,0:T(8,128)} %param.13) | copy-start | bytes 393220
  8.2 14.3 %all-to-all-start = ((bf16[4,2,40960]{2,1,0:T(2,128)(2,1)}), bf16[4,2,40960]{2,1,0:T(2,128)(2,1)S(1)}, u32[]{:S(2)}, u32[]{:S(2)}) async-start(bf16[4,2,40960]{2,1,0:T(2,128)(2,1)} %reshape.435), calls=%async_computation | async-start | bytes 1310720 | tf_op jit(solution)/shard_map/all_to_all | solution.py:91
  24.0 13.2 %copy-start.2 = (bf16[4,1,81920]{2,0,1:T(4,128)(2,1)}, bf16[4,1,81920]{2,0,1:T(4,128)(2,1)S(1)}, u32[]{:S(2)}) copy-start(bf16[4,1,81920]{2,0,1:T(4,128)(2,1)S(1)} %copy.148) | copy-start | bytes 1966084
  26.4 68.3 %all-to-all-start.1 = ((bf16[32,64,1024]{2,1,0:T(8,128)(2,1)}), bf16[32,64,1024]{2,1,0:T(8,128)(2,1)}, u32[]{:S(2)}, u32[]{:S(2)}) async-start(bf16[32,64,1024]{2,1,0:T(8,128)(2,1)} %broadcast_in_dim.188), calls=%async_computation.1 | async-start | bytes 8388608 | tf_op jit(solution)/shard_map/all_to_all | solution.py:19
  101.6 6.0 copy-start.8
  101.6 6.3 %copy-start = (bf16[256,2048]{1,0:T(8,128)(2,1)S(1)}, bf16[256,2048]{1,0:T(8,128)(2,1)}, u32[]{:S(2)}) copy-start(bf16[256,2048]{1,0:T(8,128)(2,1)} %param.11) | copy-start | bytes 3145732
  101.6 258.6 %all-to-all-start.3 = ((bf16[32,64,3584]{2,1,0:T(8,128)(2,1)}), bf16[32,64,3584]{2,1,0:T(8,128)(2,1)}, u32[]{:S(2)}, u32[]{:S(2)}) async-start(bf16[32,64,3584]{2,1,0:T(8,128)(2,1)} %stack.8), calls=%async_computation.3 | async-start | bytes 29360128 | tf_op jit(solution)/shard_map/all_to_all | solution.py:119
  119.1 217.8 %collective-permute-start.1 = (bf16[2,4,256,128]{2,3,1,0:T(8,128)(2,1)S(1)}, bf16[2,4,256,128]{2,3,1,0:T(8,128)(2,1)}, u32[]{:S(2)}, u32[]{:S(2)}) collective-permute-start(bf16[2,4,256,128]{2,3,1,0:T(8,128)(2,1)S(1)} %maximum_bitcast_fusion.1), channel_id=1, source_target_pairs={{0,32},{4,36},{8,40},{12,44},{16,48},{20,52},{24,56},{28,60},{32,6... | collective-permute-start | bytes 1572872 | tf_op jit(solution)/shard_map/ppermute | solution.py:13
  122.9 225.3 %collective-permute-start = (bf16[2,4,256,128]{2,3,1,0:T(8,128)(2,1)S(1)}, bf16[2,4,256,128]{2,3,1,0:T(8,128)(2,1)S(1)}, u32[]{:S(2)}, u32[]{:S(2)}) collective-permute-start(bf16[2,4,256,128]{2,3,1,0:T(8,128)(2,1)S(1)} %maximum_bitcast_fusion.1), channel_id=1, source_target_pairs={{0,64},{4,68},{8,72},{12,76},{16,80},{20,84},{24,88},{28,92},{32,9... | collective-permute-start | bytes 1572872 | tf_op jit(solution)/shard_map/ppermute | solution.py:13
  360.2 98.3 %all-to-all-start.2 = ((bf16[8,2,2,4,256,128]{5,4,3,2,1,0:T(8,128)(2,1)}), bf16[8,2,2,4,256,128]{5,4,3,2,1,0:T(8,128)(2,1)}, u32[]{:S(2)}, u32[]{:S(2)}) async-start(bf16[8,2,2,4,256,128]{5,4,3,2,1,0:T(8,128)(2,1)} %pad_maximum_fusion), calls=%async_computation.2 | async-start | bytes 16777216 | tf_op jit(solution)/shard_map/all_to_all | solution.py:161
  366.4 21.1 %collective-permute-start.2 = (bf16[64,2048]{1,0:T(8,128)(2,1)S(1)}, bf16[64,2048]{1,0:T(8,128)(2,1)S(1)}, u32[]{:S(2)}, u32[]{:S(2)}) collective-permute-start(bf16[64,2048]{1,0:T(8,128)(2,1)S(1)} %bitcast.144), channel_id=1, source_target_pairs={{0,0},{1,32},{2,64},{3,96},{32,1},{33,33},{34,65},{35,97},{64,2},{... | collective-permute-start | bytes 786440 | tf_op jit(solution)/shard_map/ppermute | solution.py:115
  460.1 62.4 %all-to-all-start.4 = ((bf16[8,64,2048]{2,1,0:T(8,128)(2,1)}), bf16[8,64,2048]{2,1,0:T(8,128)(2,1)}, u32[]{:S(2)}, u32[]{:S(2)}) async-start(bf16[8,64,2048]{2,1,0:T(8,128)(2,1)} %broadcast_in_dim.195), calls=%async_computation.4 | async-start | bytes 4194304 | tf_op jit(solution)/shard_map/all_to_all | solution.py:19
  525.9 32.7 %all-to-all-start.5 = ((bf16[4,64,2048]{2,1,0:T(8,128)(2,1)}), bf16[4,64,2048]{2,1,0:T(8,128)(2,1)S(1)}, u32[]{:S(2)}, u32[]{:S(2)}) async-start(bf16[4,64,2048]{2,1,0:T(8,128)(2,1)} %bitcast.124), calls=%async_computation.5 | async-start | bytes 2097152 | tf_op jit(solution)/shard_map/all_to_all | solution.py:26
  558.9 17.6 %copy-start.1 = (bf16[2048,1024]{1,0:T(8,128)(2,1)S(1)}, bf16[2048,1024]{1,0:T(8,128)(2,1)}, u32[]{:S(2)}) copy-start(bf16[2048,1024]{1,0:T(8,128)(2,1)} %get-tuple-element.279) | copy-start | bytes 12582916
